TPU v7x, 512 devices: a whole 4x8x8 slice. The times are simulated.
512 devices in a mesh: sub: 8 (over x, core), seq: 8 (over y), exp: 8 (over z).
Axes of the slice: x: 4, y: 8, z: 8, core: 2. Of those that a mesh axis runs over, the one named last changes fastest.
Arguments:
- node_features: bfloat16 [64, 1536, 1024], P(('sub', 'exp'), 'seq'), parts along dimension 0, may hold values from -24 to 24
- block_mask: int32 [64, 12, 12], P(('sub', 'exp')), parts along dimension 0, may hold values from 0 to 1, as said below
- w_qkv: bfloat16 [1024, 3072], P('exp', 'seq'), may hold values from -4 to 4
- w_out: bfloat16 [1024, 1024], P('seq', 'exp'), may hold values from -0.1875 to 0.1875
- norm_gain: float32 [1024], replicated, may hold values from 0.5 to 1.5
- routes: int32 [64, 1536, 2], P(('sub', 'exp'), 'seq'), parts along dimension 0, may hold values from 0 to 63, all different within a row; in each aligned block of 192 rows (0 to 191, 192 to 383, ..., all dimensions but the last counted through in order) at most 12 rows name the same one
- gates: float32 [64, 1536, 2], P(('sub', 'exp'), 'seq'), parts along dimension 0, may hold values from 0.1 to 1
- w_gate_up: bfloat16 [64, 1024, 1024], P(('seq', 'exp')), may hold values from -0.1875 to 0.1875
- w_down: bfloat16 [64, 512, 1024], P(('seq', 'exp')), may hold values from -0.25 to 0.25
Outputs:
- layer_out: bfloat16 [64, 1536, 1024], P(('sub', 'exp'), 'seq'), parts along dimension 0
There are 8 independent parts, one for each index of `sub`. A program takes and returns all parts, laid end to end along the dimension named above; an argument that names none is the same for every part. Nothing has to cross between parts.
Inputs may be any that keep to these rules, and one draw needn't show every extreme that they name: In each aligned block of 192 rows (one device's nodes, subgraphs then nodes in order) no expert is named by more than 12 of the rows' routes, a bound that some block reaches; the 2 experts of a node differ. `block_mask`: the diagonal blocks are 1.
All inputs are finite; a program needn't handle non-finite values.
Results may differ from a plain program's by a relative error of at most 0.0065.
The roundings to bfloat16 on the way count: a program that leaves them out, or rounds other values in their place, can miss the bound.
Values may be sent and summed in bfloat16 or wider, within the bound.
No kernel may reach another device: no remote copies, remote signals or barrier semaphores. Data moves between devices by JAX's collectives and lax.ppermute only.
A program may use at most 64 MiB of HBM per device.

v0:
```python
import math
import jax
import jax.numpy as jnp
from jax import lax
from jax.sharding import PartitionSpec as P

HEAD_DIM = 64
TOP = 2
BLOCK = 128


def per_device(
    node_features, block_mask, w_qkv, w_out, norm_gain, routes, gates, w_gate_up, w_down
):
    feats = node_features[0]
    node_dev, width = feats.shape
    seq_count = lax.axis_size("seq")
    exp_count = lax.axis_size("exp")
    experts = seq_count * exp_count * w_gate_up.shape[0]
    head_cols = w_qkv.shape[1]
    cols_slice = lax.all_gather(w_qkv, "exp", axis=0, tiled=True)
    out_rows = lax.all_gather(w_out[None], "exp", axis=0, tiled=True)
    out_all = lax.all_gather(out_rows[None], "seq", axis=0, tiled=True)
    me = lax.axis_index("seq")
    right = [(i, (i + 1) % seq_count) for i in range(seq_count)]
    left = [(i, (i - 1) % seq_count) for i in range(seq_count)]
    relative = [None] * seq_count
    relative[0] = feats
    moving_r, moving_l = (feats, feats)
    for step in range(1, seq_count // 2 + 1):
        moving_r = lax.ppermute(moving_r, "seq", right)
        relative[(seq_count - step) % seq_count] = moving_r
        if step < seq_count - step:
            moving_l = lax.ppermute(moving_l, "seq", left)
            relative[step] = moving_l
    stacked = jnp.stack(relative)
    order = (jnp.arange(seq_count, dtype=jnp.int32) - me) % seq_count
    gathered = jnp.take(stacked, order, axis=0).reshape(seq_count * node_dev, width)
    projected = jnp.dot(gathered, cols_slice, preferred_element_type=jnp.float32).astype(
        jnp.bfloat16
    )
    nodes = projected.shape[0]
    heads_here = head_cols // (3 * HEAD_DIM)
    split = projected.reshape(nodes, heads_here, 3, HEAD_DIM)
    query = split[:, :, 0]
    keys = split[:, :, 1]
    values = split[:, :, 2]
    col_mask = jnp.repeat(block_mask[0], BLOCK, axis=1) > 0
    span = math.gcd(nodes, 512)
    scale = 1.0 / math.sqrt(HEAD_DIM)

    def attend(index):
        start = index * span
        rows_query = lax.dynamic_slice_in_dim(query, start, span, 0)
        rows_mask = lax.dynamic_slice_in_dim(col_mask, start // BLOCK, span // BLOCK, 0)
        allowed = jnp.repeat(rows_mask, BLOCK, axis=0)
        scores = (
            jnp.einsum("qhd,khd->hqk", rows_query, keys, preferred_element_type=jnp.float32) * scale
        )
        scores = jnp.where(allowed[None], scores, -1e30)
        top = jnp.max(scores, axis=-1, keepdims=True)
        weights = jnp.exp(scores - top)
        probs = (weights / jnp.sum(weights, axis=-1, keepdims=True)).astype(jnp.bfloat16)
        return jnp.einsum("hqk,khd->qhd", probs, values, preferred_element_type=jnp.float32).astype(
            jnp.bfloat16
        )

    blocks = lax.map(attend, jnp.arange(nodes // span, dtype=jnp.int32))
    attended = blocks.reshape(nodes, heads_here * HEAD_DIM)
    node_attended = lax.all_to_all(attended, "seq", split_axis=0, concat_axis=1, tiled=True)
    out_tiles = out_all
    attn_out = jnp.einsum(
        "nsk,sekc->nec",
        node_attended.reshape(node_dev, seq_count, w_out.shape[0]),
        out_tiles,
        preferred_element_type=jnp.float32,
    )
    mixed = feats.astype(jnp.float32) + attn_out.reshape(node_dev, width)
    mean_square = jnp.mean(mixed * mixed, axis=-1, keepdims=True)
    normed = (mixed * lax.rsqrt(mean_square + 1e-06) * norm_gain).astype(jnp.bfloat16)
    capacity = 2 * TOP * node_dev // experts
    pair_routes = routes[0].reshape(node_dev * TOP)
    onehot = (pair_routes[:, None] == jnp.arange(experts, dtype=jnp.int32)).astype(jnp.int32)
    earlier = jnp.cumsum(onehot, axis=0, dtype=jnp.int32) - onehot
    slots = jnp.sum(earlier * onehot, axis=1, dtype=jnp.int32)
    position = pair_routes * capacity + slots
    outgoing = (
        jnp.zeros((experts * capacity, width), jnp.bfloat16)
        .at[position]
        .set(jnp.repeat(normed, TOP, axis=0))
    )
    outgoing = outgoing.reshape(experts, capacity, width)
    hidden_units = w_down.shape[1]
    received = lax.all_to_all(outgoing, ("seq", "exp"), split_axis=0, concat_axis=0, tiled=True)
    sources, items, columns = received.shape
    flat_rows = received.reshape(sources * items, columns)
    both = jnp.dot(flat_rows, w_gate_up[0], preferred_element_type=jnp.float32)
    hidden = (jax.nn.silu(both[:, :hidden_units]) * both[:, hidden_units:]).astype(jnp.bfloat16)
    result = jnp.dot(hidden, w_down[0], preferred_element_type=jnp.float32).astype(jnp.bfloat16)
    processed = result.reshape(sources, items, columns)
    returned = lax.all_to_all(
        processed, ("seq", "exp"), split_axis=0, concat_axis=0, tiled=True
    ).reshape(experts * capacity, width)
    picked = returned[position].astype(jnp.float32).reshape(node_dev, TOP, width)
    expert_sum = jnp.sum(picked * gates[0][:, :, None], axis=1)
    return (mixed + expert_sum).astype(jnp.bfloat16)[None]


def solution(mesh):
    in_specs = (
        P(("sub", "exp"), "seq", None),
        P(("sub", "exp"), None, None),
        P("exp", "seq"),
        P("seq", "exp"),
        P(),
        P(("sub", "exp"), "seq", None),
        P(("sub", "exp"), "seq", None),
        P(("seq", "exp"), None, None),
        P(("seq", "exp"), None, None),
    )
    out_specs = P(("sub", "exp"), "seq", None)
    return jax.shard_map(
        per_device, mesh=mesh, in_specs=in_specs, out_specs=out_specs, check_vma=False
    )
```

profile of v0, /device:TPU:26, one launch (start us, length us, event | category | flops | bytes accessed | tf_op | source)
XLA Modules:
  0.0 344.0 jit_solution(16411049561203123971)
XLA Ops:
  6.5 2.5 collective-permute-start
  9.0 4.7 %collective-permute-start.3 = (bf16[192,1024]{1,0:T(8,128)(2,1)}, bf16[192,1024]{1,0:T(8,128)(2,1)S(1)}, u32[]{:S(2)}, u32[]{:S(2)}) collective-permute-start(bf16[192,1024]{1,0:T(8,128)(2,1)} %bitcast.114), channel_id=1, source_target_pairs={{0,8},{8,16},{16,24},{24,32},{32,40},{40,48},{48,56},{56,0},{1,9},... | collective-permute-start | bytes 1179656 | tf_op jit(solution)/shard_map/ppermute | solution.py:31
  13.7 33.4 %all-gather = bf16[1024,128]{1,0:T(8,128)(2,1)} all-gather(bf16[128,128]{1,0:T(8,128)(2,1)} %param.14), channel_id=2, replica_groups=mesh['sub'=8,'seq'=8,'exp'=8] {'exp'}, dimensions={0}, use_global_device_ids=true | all-gather | bytes 294912 | tf_op jit(solution)/shard_map/all_gather | solution.py:22
  47.1 26.4 %all_gather.9 = bf16[1024,384]{1,0:T(8,128)(2,1)S(1)} all-gather(bf16[128,384]{1,0:T(8,128)(2,1)} %param.13), channel_id=1, replica_groups=mesh['sub'=8,'seq'=8,'exp'=8] {'exp'}, dimensions={0}, use_global_device_ids=true | all-gather | bytes 884736 | tf_op jit(solution)/shard_map/all_gather | solution.py:21
  73.5 3.3 collective-permute-start.4
  76.9 0.7 broadcast_compare_fusion
  77.6 2.5 collective-permute-start.1
  80.1 11.0 %collective-permute-done.4 = bf16[192,1024]{1,0:T(8,128)(2,1)} collective-permute-done((bf16[192,1024]{1,0:T(8,128)(2,1)S(1)}, bf16[192,1024]{1,0:T(8,128)(2,1)}, u32[]{:S(2)}, u32[]{:S(2)}) %collective-permute-start.4) | collective-permute-done | bytes 393248 | tf_op jit(solution)/shard_map/ppermute | solution.py:31
  91.1 4.7 %collective-permute-start.5 = (bf16[192,1024]{1,0:T(8,128)(2,1)}, bf16[192,1024]{1,0:T(8,128)(2,1)}, u32[]{:S(2)}, u32[]{:S(2)}) collective-permute-start(bf16[192,1024]{1,0:T(8,128)(2,1)} %collective-permute-done.4), channel_id=1, source_target_pairs={{0,8},{8,16},{16,24},{24,32},{32,40},{40,48},{48,56},{56,0},{1,9},... | collective-permute-start | bytes 1179656 | tf_op jit(solution)/shard_map/ppermute | solution.py:31
  95.9 0.8 copy.34
  97.3 1.8 constant_dynamic-update-slice_fusion
  99.0 1.9 collective-permute-start.2
  100.9 1.8 bitcast_dynamic-update-slice_fusion.6
  102.7 2.4 collective-permute-done.5
  105.1 5.6 %collective-permute-start.6 = (bf16[192,1024]{1,0:T(8,128)(2,1)}, bf16[192,1024]{1,0:T(8,128)(2,1)S(1)}, u32[]{:S(2)}, u32[]{:S(2)}) collective-permute-start(bf16[192,1024]{1,0:T(8,128)(2,1)} %collective-permute-done.5), channel_id=1, source_target_pairs={{0,8},{8,16},{16,24},{24,32},{32,40},{40,48},{48,56},{56,0},{1,9},... | collective-permute-start | bytes 1179656 | tf_op jit(solution)/shard_map/ppermute | solution.py:31
  110.7 1.8 bitcast_dynamic-update-slice_fusion.5
  112.5 0.8 bitcast_dynamic-update-slice_fusion.4
  113.3 3.0 collective-permute-done.6
  116.3 0.8 bitcast_dynamic-update-slice_fusion.3
  117.1 1.8 bitcast_dynamic-update-slice_fusion.2
  118.9 1.8 bitcast_dynamic-update-slice_fusion.1
  120.6 0.8 bitcast_dynamic-update-slice_fusion
  121.4 4.3 %gather_fusion = bf16[8,192,1024]{2,1,0:T(8,128)(2,1)} fusion(bf16[8,192,1024]{2,1,0:T(8,128)(2,1)} %bitcast_dynamic-update-slice_fusion, s32[1024]{0:T(1024)S(1)} %pad_clamp_fusion.1), kind=kCustom, calls=%fused_computation | custom fusion | bytes 6291488 | tf_op jit(solution)/shard_map/jit(_take)/gather | solution.py:38
  125.7 2.3 bitcast_select_fusion
  128.1 1.5 convolution_convert_fusion
  129.5 1.0 slice_bitcast_fusion
  130.5 28.2 %while.12 = (s32[]{:T(128)}, bf16[3,512,2,64]{1,3,2,0:T(8,128)(2,1)}, s32[3]{0:T(128)S(1)}, pred[12,1536]{1,0:T(8,128)(4,1)S(1)}, bf16[1536,2,64]{0,2,1:T(8,128)...) while((s32[]{:T(128)}, ...), condition=%wide.region_3.4_spmd, body=%wide.region_0.3_spmd.sunk | while | flops 618205184 | bytes 3959682 | solution.py:68
  130.5 0.6 dynamic_slice.40
  131.8 0.2 broadcast_in_dim.124
  132.1 3.4 fusion.75
  135.5 4.4 %fusion.76 = bf16[3,512,2,64]{1,3,2,0:T(8,128)(2,1)} fusion(bf16[3,512,2,64]{1,3,2,0:T(8,128)(2,1)} %get-tuple-element.174, s32[]{:T(128)} %get-tuple-element.173, bf16[1536,2,64]{0,2,1:T(8,128)(2,1)S(1)} %get-tuple-element.194, f32[2,512]{1,0:T(2,128)S(1)} %fusion.75, pred[512,1536]{1,0:T(8,128)(4,1)S(1)} %bitcast.110, ...), kind=kOutput, calls=%fused_computation.14.clone.1 | convolution fusion | flops 410585600 | bytes 1839620 | tf_op jit(solution)/shard_map/while/body/eval_jaxpr/hqk,khd->qhd/dot_general | solution.py:64
  139.9 0.6 dynamic_slice.40
  141.2 0.2 broadcast_in_dim.124
  141.5 3.4 fusion.75
  144.9 4.4 %fusion.76 = bf16[3,512,2,64]{1,3,2,0:T(8,128)(2,1)} fusion(bf16[3,512,2,64]{1,3,2,0:T(8,128)(2,1)} %get-tuple-element.174, s32[]{:T(128)} %get-tuple-element.173, bf16[1536,2,64]{0,2,1:T(8,128)(2,1)S(1)} %get-tuple-element.194, f32[2,512]{1,0:T(2,128)S(1)} %fusion.75, pred[512,1536]{1,0:T(8,128)(4,1)S(1)} %bitcast.110, ...), kind=kOutput, calls=%fused_computation.14.clone.1 | convolution fusion | flops 410585600 | bytes 1839620 | tf_op jit(solution)/shard_map/while/body/eval_jaxpr/hqk,khd->qhd/dot_general | solution.py:64
  149.3 0.6 dynamic_slice.40
  150.7 0.2 broadcast_in_dim.124
  150.9 3.4 fusion.75
  154.3 4.4 %fusion.76 = bf16[3,512,2,64]{1,3,2,0:T(8,128)(2,1)} fusion(bf16[3,512,2,64]{1,3,2,0:T(8,128)(2,1)} %get-tuple-element.174, s32[]{:T(128)} %get-tuple-element.173, bf16[1536,2,64]{0,2,1:T(8,128)(2,1)S(1)} %get-tuple-element.194, f32[2,512]{1,0:T(2,128)S(1)} %fusion.75, pred[512,1536]{1,0:T(8,128)(4,1)S(1)} %bitcast.110, ...), kind=kOutput, calls=%fused_computation.14.clone.1 | convolution fusion | flops 410585600 | bytes 1839620 | tf_op jit(solution)/shard_map/while/body/eval_jaxpr/hqk,khd->qhd/dot_general | solution.py:64
  158.7 2.2 copy.38
  160.9 1.1 reshape.189
  162.0 8.2 %all-to-all-start = ((bf16[8,192,128]{2,1,0:T(8,128)(2,1)}), bf16[8,192,128]{2,1,0:T(8,128)(2,1)S(1)}, u32[]{:S(2)}, u32[]{:S(2)}) async-start(bf16[8,192,128]{2,1,0:T(8,128)(2,1)} %reshape.189), calls=%async_computation | async-start | bytes 786432 | tf_op jit(solution)/shard_map/all_to_all | solution.py:70
  170.3 0.9 reduce-window.6
  171.2 0.2 slice_reduce_fusion
  171.9 3.9 %copy.32 = bf16[8,8,128,128]{2,3,1,0:T(8,128)(2,1)} copy(bf16[8,8,128,128]{3,2,1,0:T(8,128)(2,1)} %bitcast.112) | data formatting | bytes 4194304 | tf_op jit(solution)/shard_map/all_gather | solution.py:23
  175.8 2.9 all-to-all-done
  178.7 0.7 copy-done.2
  179.5 2.7 multiply_reduce_fusion.1
  182.3 1.3 broadcast_in_dim.87
  183.6 3.0 reshape.182
  186.6 4.0 %scatter_custom_fusion = bf16[768,1024]{1,0:T(8,128)(2,1)} fusion(s32[384]{0:T(512)S(1)} %fusion.48, bf16[384,1024]{1,0:T(8,128)(2,1)} %reshape.182, bf16[]{:T(256)} %constant.125.clone.1), kind=kCustom, calls=%fused_computation.44 | custom fusion | bytes 1573376 | tf_op jit(solution)/shard_map/scatter | solution.py:90
  190.6 3.6 %reshape.157 = bf16[64,12,1024]{2,1,0:T(8,128)(2,1)} reshape(bf16[768,1024]{1,0:T(8,128)(2,1)} %scatter_custom_fusion) | data formatting | bytes 3145728 | tf_op jit(solution)/shard_map/reshape | solution.py:92
  194.2 52.2 %all_to_all.26 = bf16[64,12,1024]{2,1,0:T(8,128)(2,1)} all-to-all(bf16[64,12,1024]{2,1,0:T(8,128)(2,1)} %reshape.157), channel_id=1, replica_groups=mesh['sub'=8,'seq'=8,'exp'=8] {'seq','exp'}, dimensions={0} | all-to-all | bytes 3145728 | tf_op jit(solution)/shard_map/all_to_all | solution.py:94
  246.3 3.6 %reshape.158 = bf16[768,1024]{1,0:T(8,128)(2,1)} reshape(bf16[64,12,1024]{2,1,0:T(8,128)(2,1)} %all_to_all.26) | data formatting | bytes 3145728 | tf_op jit(solution)/shard_map/reshape | solution.py:96
  250.0 3.3 fusion.33
  253.3 2.2 convolution_convert_fusion.1
  255.4 3.6 %reshape.159 = bf16[64,12,1024]{2,1,0:T(8,128)(2,1)} reshape(bf16[768,1024]{1,0:T(8,128)(2,1)} %convolution_convert_fusion.1) | data formatting | bytes 3145728 | tf_op jit(solution)/shard_map/reshape | solution.py:100
  259.0 9.6 %all-to-all-start.2 = ((bf16[64,12,1024]{2,1,0:T(8,128)(2,1)}), bf16[64,12,1024]{2,1,0:T(8,128)(2,1)}, u32[]{:S(2)}, u32[]{:S(2)}) async-start(bf16[64,12,1024]{2,1,0:T(8,128)(2,1)} %reshape.159), calls=%async_computation.2 | async-start | bytes 4194304 | tf_op jit(solution)/shard_map/all_to_all | solution.py:101
  268.8 52.5 %all-to-all-done.2 = bf16[64,12,1024]{2,1,0:T(8,128)(2,1)} async-done(((bf16[64,12,1024]{2,1,0:T(8,128)(2,1)}), bf16[64,12,1024]{2,1,0:T(8,128)(2,1)}, u32[]{:S(2)}, u32[]{:S(2)}) %all-to-all-start.2) | async-done | bytes 1572896 | tf_op jit(solution)/shard_map/all_to_all | solution.py:101
  321.3 3.6 %reshape.160 = bf16[768,1024]{1,0:T(8,128)(2,1)} reshape(bf16[64,12,1024]{2,1,0:T(8,128)(2,1)} %all-to-all-done.2) | data formatting | bytes 3145728 | tf_op jit(solution)/shard_map/reshape | solution.py:103
  324.9 5.0 %gather_fusion.1 = bf16[384,1024]{1,0:T(8,128)(2,1)} fusion(bf16[768,1024]{1,0:T(8,128)(2,1)} %reshape.160, s32[1024]{0:T(1024)S(1)} %pad_clamp_fusion), kind=kCustom, calls=%fused_computation.1 | custom fusion | bytes 1574400 | tf_op jit(solution)/shard_map/gather | solution.py:104
  329.9 3.0 reshape.161
  332.8 3.4 %multiply_reduce_fusion = f32[192,1024]{1,0:T(8,128)S(1)} fusion(f32[192,2,1024]{2,1,0:T(2,128)} %reshape.161, f32[192,2]{1,0:T(8,128)S(1)} %copy.37), kind=kLoop, calls=%fused_computation.36 | loop fusion | flops 589824 | bytes 2360832 | tf_op jit(solution)/shard_map/reduce_sum | solution.py:105
  336.3 0.8 fusion.42
  (47 shorter events, 1.5 us)
Async XLA Ops:
  6.5 243.4 %copy-start = (bf16[1,1024,1024]{2,1,0:T(8,128)(2,1)S(1)}, bf16[1,1024,1024]{2,1,0:T(8,128)(2,1)}, u32[]{:S(2)}) copy-start(bf16[1,1024,1024]{2,1,0:T(8,128)(2,1)} %param.18) | copy-start | bytes 6291460
  6.5 165.3 %all-gather.4.cloned.1.call-start = ((), (), s32[]{:S(2)}) async-start(), calls=%async_computation.3 | async-start | bytes 2359296 | tf_op jit(solution)/shard_map/all_gather | solution.py:23
  6.5 71.1 %collective-permute-start = (bf16[192,1024]{1,0:T(8,128)(2,1)}, bf16[192,1024]{1,0:T(8,128)(2,1)}, u32[]{:S(2)}, u32[]{:S(2)}) collective-permute-start(bf16[192,1024]{1,0:T(8,128)(2,1)} %bitcast.113), channel_id=1, source_target_pairs={{0,56},{8,0},{16,8},{24,16},{32,24},{40,32},{48,40},{56,48},{1,57}... | collective-permute-start | bytes 1179656 | tf_op jit(solution)/shard_map/ppermute | solution.py:34
  9.0 64.5 %collective-permute-start.3 = (bf16[192,1024]{1,0:T(8,128)(2,1)}, bf16[192,1024]{1,0:T(8,128)(2,1)S(1)}, u32[]{:S(2)}, u32[]{:S(2)}) collective-permute-start(bf16[192,1024]{1,0:T(8,128)(2,1)} %bitcast.114), channel_id=1, source_target_pairs={{0,8},{8,16},{16,24},{24,32},{32,40},{40,48},{48,56},{56,0},{1,9},... | collective-permute-start | bytes 1179656 | tf_op jit(solution)/shard_map/ppermute | solution.py:31
  73.5 17.6 %collective-permute-start.4 = (bf16[192,1024]{1,0:T(8,128)(2,1)S(1)}, bf16[192,1024]{1,0:T(8,128)(2,1)}, u32[]{:S(2)}, u32[]{:S(2)}) collective-permute-start(bf16[192,1024]{1,0:T(8,128)(2,1)S(1)} %collective-permute-done.3), channel_id=1, source_target_pairs={{0,8},{8,16},{16,24},{24,32},{32,40},{40,48},{48,56},{56,0},{1,9},... | collective-permute-start | bytes 1179656 | tf_op jit(solution)/shard_map/ppermute | solution.py:31
  77.6 21.4 %collective-permute-start.1 = (bf16[192,1024]{1,0:T(8,128)(2,1)}, bf16[192,1024]{1,0:T(8,128)(2,1)}, u32[]{:S(2)}, u32[]{:S(2)}) collective-permute-start(bf16[192,1024]{1,0:T(8,128)(2,1)} %collective-permute-done), channel_id=1, source_target_pairs={{0,56},{8,0},{16,8},{24,16},{32,24},{40,32},{48,40},{56,48},{1,57}... | collective-permute-start | bytes 1179656 | tf_op jit(solution)/shard_map/ppermute | solution.py:34
  91.1 14.0 %collective-permute-start.5 = (bf16[192,1024]{1,0:T(8,128)(2,1)}, bf16[192,1024]{1,0:T(8,128)(2,1)}, u32[]{:S(2)}, u32[]{:S(2)}) collective-permute-start(bf16[192,1024]{1,0:T(8,128)(2,1)} %collective-permute-done.4), channel_id=1, source_target_pairs={{0,8},{8,16},{16,24},{24,32},{32,40},{40,48},{48,56},{56,0},{1,9},... | collective-permute-start | bytes 1179656 | tf_op jit(solution)/shard_map/ppermute | solution.py:31
  99.0 13.4 %collective-permute-start.2 = (bf16[192,1024]{1,0:T(8,128)(2,1)}, bf16[192,1024]{1,0:T(8,128)(2,1)S(1)}, u32[]{:S(2)}, u32[]{:S(2)}) collective-permute-start(bf16[192,1024]{1,0:T(8,128)(2,1)} %collective-permute-done.1), channel_id=1, source_target_pairs={{0,56},{8,0},{16,8},{24,16},{32,24},{40,32},{48,40},{56,48},{1,57}... | collective-permute-start | bytes 1179656 | tf_op jit(solution)/shard_map/ppermute | solution.py:34
  105.1 11.2 %collective-permute-start.6 = (bf16[192,1024]{1,0:T(8,128)(2,1)}, bf16[192,1024]{1,0:T(8,128)(2,1)S(1)}, u32[]{:S(2)}, u32[]{:S(2)}) collective-permute-start(bf16[192,1024]{1,0:T(8,128)(2,1)} %collective-permute-done.5), channel_id=1, source_target_pairs={{0,8},{8,16},{16,24},{24,32},{32,40},{40,48},{48,56},{56,0},{1,9},... | collective-permute-start | bytes 1179656 | tf_op jit(solution)/shard_map/ppermute | solution.py:31
  158.7 12.7 %copy-start.3 = (s32[1,192,2]{1,2,0:T(2,128)S(1)}, s32[1,192,2]{1,2,0:T(2,128)}, u32[]{:S(2)}) copy-start(s32[1,192,2]{1,2,0:T(2,128)} %param.16) | copy-start | bytes 4612
  162.0 17.5 %copy-start.1 = (bf16[1,192,1024]{2,1,0:T(8,128)(2,1)S(1)}, bf16[1,192,1024]{2,1,0:T(8,128)(2,1)}, u32[]{:S(2)}) copy-start(bf16[1,192,1024]{2,1,0:T(8,128)(2,1)} %param.11) | copy-start | bytes 1179652
  162.0 16.7 %all-to-all-start = ((bf16[8,192,128]{2,1,0:T(8,128)(2,1)}), bf16[8,192,128]{2,1,0:T(8,128)(2,1)S(1)}, u32[]{:S(2)}, u32[]{:S(2)}) async-start(bf16[8,192,128]{2,1,0:T(8,128)(2,1)} %reshape.189), calls=%async_computation | async-start | bytes 786432 | tf_op jit(solution)/shard_map/all_to_all | solution.py:70
  171.9 10.3 %copy-start.4 = (f32[1024]{0:T(1024)S(1)}, f32[1024]{0:T(1024)}, u32[]{:S(2)}) copy-start(f32[1024]{0:T(1024)} %param.15) | copy-start | bytes 12292
  178.7 0.7 copy-start.2
  250.0 3.3 copy-start.6
  255.4 13.2 %copy-start.5 = (f32[1,192,2]{1,2,0:T(2,128)S(1)}, f32[1,192,2]{1,2,0:T(2,128)}, u32[]{:S(2)}) copy-start(f32[1,192,2]{1,2,0:T(2,128)} %param.17) | copy-start | bytes 4612
  259.0 62.2 %all-to-all-start.2 = ((bf16[64,12,1024]{2,1,0:T(8,128)(2,1)}), bf16[64,12,1024]{2,1,0:T(8,128)(2,1)}, u32[]{:S(2)}, u32[]{:S(2)}) async-start(bf16[64,12,1024]{2,1,0:T(8,128)(2,1)} %reshape.159), calls=%async_computation.2 | async-start | bytes 4194304 | tf_op jit(solution)/shard_map/all_to_all | solution.py:101
Sparse Core Ops, SparseCore 0:
  47.2 43.0 all-gather.3
where the time goes:
time: 346 us; the launch traced here: 344 us
  blocking collectives  112 us (32%)
  waiting for transfers between devices  71.8 us (21%)
  local copies, waits for them, and re-layouts  59.7 us (17%)
  starting transfers between devices  43 us (12%)
  matrix products  33.1 us (10%)
  between operations  13.7 us (4%)
  other arithmetic  8.59 us (2%)
    all_to_all x1, waiting for transfers between devices, per_device(): lax.all_to_all(processed, ('seq', 'exp'), split_axis=0, concat_axis=0, ti...  52.5 us
    all_to_all x1, blocking collectives, per_device(): lax.all_to_all(outgoing, ('seq', 'exp'), split_axis=0, concat_axis=0, til...  52.2 us
    all_gather x1, blocking collectives, per_device(): out_rows = lax.all_gather(w_out[None], 'exp', axis=0, tiled=True)  33.4 us
    all_gather x1, blocking collectives, per_device(): cols_slice = lax.all_gather(w_qkv, 'exp', axis=0, tiled=True)  26.4 us
    ppermute x4, starting transfers between devices, per_device(): moving_r = lax.ppermute(moving_r, 'seq', right)  18.3 us
    ppermute x4, waiting for transfers between devices, per_device(): moving_r = lax.ppermute(moving_r, 'seq', right)  16.4 us
    dot_general x3, matrix products, attend(): jnp.einsum('hqk,khd->qhd', probs, values, preferred_element_type=jnp.floa...  13.2 us
    unnamed x25, local copies, waits for them, and re-layouts  12 us
  transfers between devices with their start and end apart: 10, of which 5 were waited for; matrix products, arithmetic and copies ran while one was open for 17% of the time, Pallas kernels for 0%

commit v1 on v0

--- a/solution.py
+++ b/solution.py
@@ -3,6 +3,7 @@
 import jax.numpy as jnp
 from jax import lax
 from jax.sharding import PartitionSpec as P
+from jax.lax import all_to_all, axis_size
 
 HEAD_DIM = 64
 TOP = 2
@@ -67,7 +68,9 @@
 
     blocks = lax.map(attend, jnp.arange(nodes // span, dtype=jnp.int32))
     attended = blocks.reshape(nodes, heads_here * HEAD_DIM)
-    node_attended = lax.all_to_all(attended, "seq", split_axis=0, concat_axis=1, tiled=True)
+    node_attended = jnp.concatenate(
+        all_to_all(jnp.stack(jnp.split(attended, axis_size("seq"), 0), 0), "seq", 0, 0), 1
+    )
     out_tiles = out_all
     attn_out = jnp.einsum(
         "nsk,sekc->nec",

time: 346 us -> 357 us (1.032)
  local copies, waits for them, and re-layouts: 59.7 us -> 68.1 us
    unnamed x25 -> x36, local copies, waits for them, and re-layouts: 12 us -> 21.3 us
    all_to_all x1, waiting for transfers between devices: 2.89 us -> 6.87 us  [per_device(): all_to_all(jnp.stack(jnp.split(attended, axis_size('seq'), 0), 0), 'seq',...]
    all_gather x1 -> x0, local copies, waits for them, and re-layouts: 3.94 us -> none  [per_device(): out_all = lax.all_gather(out_rows[None], 'seq', axis=0, tiled=True)]
    reshape x0 -> x3, local copies, waits for them, and re-layouts: none -> 3.77 us  [the longest x2 2.51 us: per_device(): attended = blocks.reshape(nodes, heads_here * HEAD_DIM)]
  transfers between devices with their start and end apart: 10 -> 10, of which waited for: 5 -> 5; matrix products, arithmetic and copies ran while one was open for 17% -> 19% of each run, Pallas kernels for 0% -> 0%
where the time goes in v1:
time: 357 us; the launch traced here: 355 us
  blocking collectives  115 us (32%)
  waiting for transfers between devices  72.6 us (20%)
  local copies, waits for them, and re-layouts  68.1 us (19%)
  starting transfers between devices  40 us (11%)
  matrix products  33 us (9%)
  between operations  13.7 us (4%)
  other arithmetic  10.7 us (3%)
    all_to_all x1, blocking collectives, per_device(): lax.all_to_all(outgoing, ('seq', 'exp'), split_axis=0, concat_axis=0, til...  53 us
    all_to_all x1, waiting for transfers between devices, per_device(): lax.all_to_all(processed, ('seq', 'exp'), split_axis=0, concat_axis=0, ti...  50.2 us
    all_gather x1, blocking collectives, per_device(): out_rows = lax.all_gather(w_out[None], 'exp', axis=0, tiled=True)  33.4 us
    all_gather x1, blocking collectives, per_device(): cols_slice = lax.all_gather(w_qkv, 'exp', axis=0, tiled=True)  28.2 us
    unnamed x36, local copies, waits for them, and re-layouts  21.3 us
    ppermute x4, starting transfers between devices, per_device(): moving_r = lax.ppermute(moving_r, 'seq', right)  15.6 us
    ppermute x4, waiting for transfers between devices, per_device(): moving_r = lax.ppermute(moving_r, 'seq', right)  15.5 us
    dot_general x3, matrix products, attend(): jnp.einsum('hqk,khd->qhd', probs, values, preferred_element_type=jnp.floa...  13.2 us
  transfers between devices with their start and end apart: 10, of which 5 were waited for; matrix products, arithmetic and copies ran while one was open for 19% of the time, Pallas kernels for 0%

profile of v1, /device:TPU:26, one launch (start us, length us, event | category | flops | bytes accessed | tf_op | source)
XLA Modules:
  0.0 354.7 jit_solution(11602957375994477061)
XLA Ops:
  6.5 2.5 collective-permute-start
  9.0 4.7 %collective-permute-start.3 = (bf16[192,1024]{1,0:T(8,128)(2,1)}, bf16[192,1024]{1,0:T(8,128)(2,1)S(1)}, u32[]{:S(2)}, u32[]{:S(2)}) collective-permute-start(bf16[192,1024]{1,0:T(8,128)(2,1)} %bitcast.162), channel_id=1, source_target_pairs={{0,8},{8,16},{16,24},{24,32},{32,40},{40,48},{48,56},{56,0},{1,9},... | collective-permute-start | bytes 1179656 | tf_op jit(solution)/shard_map/ppermute | solution.py:32
  13.7 33.4 %all-gather = bf16[1024,128]{1,0:T(8,128)(2,1)} all-gather(bf16[128,128]{1,0:T(8,128)(2,1)} %param.14), channel_id=2, replica_groups=mesh['sub'=8,'seq'=8,'exp'=8] {'exp'}, dimensions={0}, use_global_device_ids=true | all-gather | bytes 294912 | tf_op jit(solution)/shard_map/all_gather | solution.py:23
  47.1 28.2 %all_gather.9 = bf16[1024,384]{1,0:T(8,128)(2,1)} all-gather(bf16[128,384]{1,0:T(8,128)(2,1)} %param.13), channel_id=1, replica_groups=mesh['sub'=8,'seq'=8,'exp'=8] {'exp'}, dimensions={0}, use_global_device_ids=true | all-gather | bytes 884736 | tf_op jit(solution)/shard_map/all_gather | solution.py:22
  75.4 3.5 collective-permute-start.4
  78.9 2.0 convert_bitcast_fusion
  80.8 2.3 collective-permute-start.1
  83.9 8.1 %collective-permute-done.4 = bf16[192,1024]{1,0:T(8,128)(2,1)} collective-permute-done((bf16[192,1024]{1,0:T(8,128)(2,1)S(1)}, bf16[192,1024]{1,0:T(8,128)(2,1)}, u32[]{:S(2)}, u32[]{:S(2)}) %collective-permute-start.4) | collective-permute-done | bytes 393248 | tf_op jit(solution)/shard_map/ppermute | solution.py:32
  92.0 3.5 collective-permute-start.5
  95.6 0.8 copy.51
  97.0 1.1 copy.67
  98.1 2.3 collective-permute-start.2
  100.4 1.8 bitcast_dynamic-update-slice_fusion.6
  102.2 3.9 %collective-permute-done.5 = bf16[192,1024]{1,0:T(8,128)(2,1)} collective-permute-done((bf16[192,1024]{1,0:T(8,128)(2,1)}, bf16[192,1024]{1,0:T(8,128)(2,1)}, u32[]{:S(2)}, u32[]{:S(2)}) %collective-permute-start.5) | collective-permute-done | bytes 393248 | tf_op jit(solution)/shard_map/ppermute | solution.py:32
  106.1 3.9 %collective-permute-start.6 = (bf16[192,1024]{1,0:T(8,128)(2,1)}, bf16[192,1024]{1,0:T(8,128)(2,1)S(1)}, u32[]{:S(2)}, u32[]{:S(2)}) collective-permute-start(bf16[192,1024]{1,0:T(8,128)(2,1)} %collective-permute-done.5), channel_id=1, source_target_pairs={{0,8},{8,16},{16,24},{24,32},{32,40},{40,48},{48,56},{56,0},{1,9},... | collective-permute-start | bytes 1179656 | tf_op jit(solution)/shard_map/ppermute | solution.py:32
  109.9 1.8 bitcast_dynamic-update-slice_fusion.5
  111.7 0.8 bitcast_dynamic-update-slice_fusion.4
  112.5 3.4 collective-permute-done.6
  115.9 0.8 bitcast_dynamic-update-slice_fusion.3
  116.7 1.8 bitcast_dynamic-update-slice_fusion.2
  118.5 1.8 bitcast_dynamic-update-slice_fusion.1
  120.3 0.8 bitcast_dynamic-update-slice_fusion
  121.0 4.3 %gather_fusion = bf16[8,192,1024]{2,1,0:T(8,128)(2,1)} fusion(bf16[8,192,1024]{2,1,0:T(8,128)(2,1)} %bitcast_dynamic-update-slice_fusion, s32[1024]{0:T(1024)S(1)} %pad_clamp_fusion.1), kind=kCustom, calls=%fused_computation | custom fusion | bytes 6291488 | tf_op jit(solution)/shard_map/jit(_take)/gather | solution.py:39
  125.4 2.4 bitcast_select_fusion
  127.8 1.4 convolution_convert_fusion
  129.3 1.0 slice_bitcast_fusion
  130.2 27.9 %while.12 = (s32[]{:T(128)}, bf16[3,512,2,64]{1,3,2,0:T(8,128)(2,1)}, s32[3]{0:T(128)S(1)}, pred[12,1536]{1,0:T(8,128)(4,1)S(1)}, bf16[1536,2,64]{0,2,1:T(8,128)...) while((s32[]{:T(128)}, ...), condition=%wide.region_3.4_spmd, body=%wide.region_0.3_spmd.sunk | while | flops 618205184 | bytes 3959682 | solution.py:69
  131.7 3.4 fusion.90
  135.1 4.4 %fusion.91 = bf16[3,512,2,64]{1,3,2,0:T(8,128)(2,1)} fusion(bf16[3,512,2,64]{1,3,2,0:T(8,128)(2,1)} %get-tuple-element.176, s32[]{:T(128)} %get-tuple-element.175, bf16[1536,2,64]{0,2,1:T(8,128)(2,1)S(1)} %get-tuple-element.196, f32[2,512]{1,0:T(2,128)S(1)} %fusion.90, pred[512,1536]{1,0:T(8,128)(4,1)S(1)} %bitcast.159, ...), kind=kOutput, calls=%fused_computation.14.clone.1 | convolution fusion | flops 410585600 | bytes 1839620 | tf_op jit(solution)/shard_map/while/body/eval_jaxpr/hqk,khd->qhd/dot_general | solution.py:65
  141.0 3.4 fusion.90
  144.4 4.4 %fusion.91 = bf16[3,512,2,64]{1,3,2,0:T(8,128)(2,1)} fusion(bf16[3,512,2,64]{1,3,2,0:T(8,128)(2,1)} %get-tuple-element.176, s32[]{:T(128)} %get-tuple-element.175, bf16[1536,2,64]{0,2,1:T(8,128)(2,1)S(1)} %get-tuple-element.196, f32[2,512]{1,0:T(2,128)S(1)} %fusion.90, pred[512,1536]{1,0:T(8,128)(4,1)S(1)} %bitcast.159, ...), kind=kOutput, calls=%fused_computation.14.clone.1 | convolution fusion | flops 410585600 | bytes 1839620 | tf_op jit(solution)/shard_map/while/body/eval_jaxpr/hqk,khd->qhd/dot_general | solution.py:65
  150.3 3.4 fusion.90
  153.7 4.4 %fusion.91 = bf16[3,512,2,64]{1,3,2,0:T(8,128)(2,1)} fusion(bf16[3,512,2,64]{1,3,2,0:T(8,128)(2,1)} %get-tuple-element.176, s32[]{:T(128)} %get-tuple-element.175, bf16[1536,2,64]{0,2,1:T(8,128)(2,1)S(1)} %get-tuple-element.196, f32[2,512]{1,0:T(2,128)S(1)} %fusion.90, pred[512,1536]{1,0:T(8,128)(4,1)S(1)} %bitcast.159, ...), kind=kOutput, calls=%fused_computation.14.clone.1 | convolution fusion | flops 410585600 | bytes 1839620 | tf_op jit(solution)/shard_map/while/body/eval_jaxpr/hqk,khd->qhd/dot_general | solution.py:65
  158.1 2.2 copy.58
  162.0 1.5 fusion.60
  163.5 1.4 fusion.59
  164.9 1.4 fusion.58
  166.3 1.4 fusion.57
  167.7 1.4 fusion.56
  169.1 1.4 fusion.55
  170.6 1.4 fusion.54
  172.0 7.7 %all-to-all-start = ((bf16[8,192,128]{2,1,0:T(8,128)(2,1)}), bf16[8,192,128]{2,1,0:T(8,128)(2,1)S(1)}, u32[]{:S(2)}, u32[]{:S(2)}) async-start(bf16[8,192,128]{2,1,0:T(8,128)(2,1)} %fusion.54), calls=%async_computation | async-start | bytes 786432 | tf_op jit(solution)/shard_map/all_to_all | solution.py:72
  179.7 0.9 reduce-window.6
  181.3 6.9 %all-to-all-done = bf16[8,192,128]{2,1,0:T(8,128)(2,1)S(1)} async-done(((bf16[8,192,128]{2,1,0:T(8,128)(2,1)}), bf16[8,192,128]{2,1,0:T(8,128)(2,1)S(1)}, u32[]{:S(2)}, u32[]{:S(2)}) %all-to-all-start) | async-done | bytes 393248 | tf_op jit(solution)/shard_map/all_to_all | solution.py:72
  188.2 0.7 copy-done.2
  188.9 2.6 fusion.44
  191.7 1.3 broadcast_in_dim.85
  193.0 3.0 reshape.194
  196.0 4.0 %scatter_custom_fusion = bf16[768,1024]{1,0:T(8,128)(2,1)} fusion(s32[384]{0:T(512)S(1)} %fusion.62, bf16[384,1024]{1,0:T(8,128)(2,1)} %reshape.194, bf16[]{:T(256)} %constant.125.clone.1), kind=kCustom, calls=%fused_computation.50 | custom fusion | bytes 1573376 | tf_op jit(solution)/shard_map/scatter | solution.py:93
  199.9 3.6 %reshape.168 = bf16[64,12,1024]{2,1,0:T(8,128)(2,1)} reshape(bf16[768,1024]{1,0:T(8,128)(2,1)} %scatter_custom_fusion) | data formatting | bytes 3145728 | tf_op jit(solution)/shard_map/reshape | solution.py:95
  203.6 53.0 %all_to_all.15 = bf16[64,12,1024]{2,1,0:T(8,128)(2,1)} all-to-all(bf16[64,12,1024]{2,1,0:T(8,128)(2,1)} %reshape.168), channel_id=1, replica_groups=mesh['sub'=8,'seq'=8,'exp'=8] {'seq','exp'}, dimensions={0} | all-to-all | bytes 3145728 | tf_op jit(solution)/shard_map/all_to_all | solution.py:97
  256.6 3.6 %reshape.169 = bf16[768,1024]{1,0:T(8,128)(2,1)} reshape(bf16[64,12,1024]{2,1,0:T(8,128)(2,1)} %all_to_all.15) | data formatting | bytes 3145728 | tf_op jit(solution)/shard_map/reshape | solution.py:99
  260.2 3.3 fusion.33
  263.5 2.2 convolution_convert_fusion.1
  265.7 3.6 %reshape.170 = bf16[64,12,1024]{2,1,0:T(8,128)(2,1)} reshape(bf16[768,1024]{1,0:T(8,128)(2,1)} %convolution_convert_fusion.1) | data formatting | bytes 3145728 | tf_op jit(solution)/shard_map/reshape | solution.py:103
  269.3 9.6 %all-to-all-start.2 = ((bf16[64,12,1024]{2,1,0:T(8,128)(2,1)}), bf16[64,12,1024]{2,1,0:T(8,128)(2,1)}, u32[]{:S(2)}, u32[]{:S(2)}) async-start(bf16[64,12,1024]{2,1,0:T(8,128)(2,1)} %reshape.170), calls=%async_computation.2 | async-start | bytes 4194304 | tf_op jit(solution)/shard_map/all_to_all | solution.py:104
  279.1 1.3 copy.49
  280.4 1.3 reshape.164
  281.7 50.2 %all-to-all-done.2 = bf16[64,12,1024]{2,1,0:T(8,128)(2,1)} async-done(((bf16[64,12,1024]{2,1,0:T(8,128)(2,1)}), bf16[64,12,1024]{2,1,0:T(8,128)(2,1)}, u32[]{:S(2)}, u32[]{:S(2)}) %all-to-all-start.2) | async-done | bytes 1572896 | tf_op jit(solution)/shard_map/all_to_all | solution.py:104
  331.9 3.6 %reshape.171 = bf16[768,1024]{1,0:T(8,128)(2,1)} reshape(bf16[64,12,1024]{2,1,0:T(8,128)(2,1)} %all-to-all-done.2) | data formatting | bytes 3145728 | tf_op jit(solution)/shard_map/reshape | solution.py:106
  335.5 5.0 %gather_fusion.1 = bf16[384,1024]{1,0:T(8,128)(2,1)} fusion(bf16[768,1024]{1,0:T(8,128)(2,1)} %reshape.171, s32[1024]{0:T(1024)S(1)} %pad_clamp_fusion), kind=kCustom, calls=%fused_computation.1 | custom fusion | bytes 1574400 | tf_op jit(solution)/shard_map/gather | solution.py:107
  340.5 3.0 reshape.173
  343.5 3.4 multiply_reduce_fusion
  346.9 0.9 fusion.38
  (61 shorter events, 6.5 us)
Async XLA Ops:
  6.5 253.7 %copy-start = (bf16[1,1024,1024]{2,1,0:T(8,128)(2,1)S(1)}, bf16[1,1024,1024]{2,1,0:T(8,128)(2,1)}, u32[]{:S(2)}) copy-start(bf16[1,1024,1024]{2,1,0:T(8,128)(2,1)} %param.18) | copy-start | bytes 6291460
  6.5 181.6 %all-gather.4.cloned.1.call-start = ((), (), s32[]{:S(2)}) async-start(), calls=%async_computation.3 | async-start | bytes 2359296 | tf_op jit(solution)/shard_map/all_gather | solution.py:24
  6.5 74.3 %collective-permute-start = (bf16[192,1024]{1,0:T(8,128)(2,1)}, bf16[192,1024]{1,0:T(8,128)(2,1)}, u32[]{:S(2)}, u32[]{:S(2)}) collective-permute-start(bf16[192,1024]{1,0:T(8,128)(2,1)} %bitcast.161), channel_id=1, source_target_pairs={{0,56},{8,0},{16,8},{24,16},{32,24},{40,32},{48,40},{56,48},{1,57}... | collective-permute-start | bytes 1179656 | tf_op jit(solution)/shard_map/ppermute | solution.py:35
  9.0 66.3 %collective-permute-start.3 = (bf16[192,1024]{1,0:T(8,128)(2,1)}, bf16[192,1024]{1,0:T(8,128)(2,1)S(1)}, u32[]{:S(2)}, u32[]{:S(2)}) collective-permute-start(bf16[192,1024]{1,0:T(8,128)(2,1)} %bitcast.162), channel_id=1, source_target_pairs={{0,8},{8,16},{16,24},{24,32},{32,40},{40,48},{48,56},{56,0},{1,9},... | collective-permute-start | bytes 1179656 | tf_op jit(solution)/shard_map/ppermute | solution.py:32
  75.4 16.7 %collective-permute-start.4 = (bf16[192,1024]{1,0:T(8,128)(2,1)S(1)}, bf16[192,1024]{1,0:T(8,128)(2,1)}, u32[]{:S(2)}, u32[]{:S(2)}) collective-permute-start(bf16[192,1024]{1,0:T(8,128)(2,1)S(1)} %collective-permute-done.3), channel_id=1, source_target_pairs={{0,8},{8,16},{16,24},{24,32},{32,40},{40,48},{48,56},{56,0},{1,9},... | collective-permute-start | bytes 1179656 | tf_op jit(solution)/shard_map/ppermute | solution.py:32
  80.8 17.2 %collective-permute-start.1 = (bf16[192,1024]{1,0:T(8,128)(2,1)}, bf16[192,1024]{1,0:T(8,128)(2,1)}, u32[]{:S(2)}, u32[]{:S(2)}) collective-permute-start(bf16[192,1024]{1,0:T(8,128)(2,1)} %collective-permute-done), channel_id=1, source_target_pairs={{0,56},{8,0},{16,8},{24,16},{32,24},{40,32},{48,40},{56,48},{1,57}... | collective-permute-start | bytes 1179656 | tf_op jit(solution)/shard_map/ppermute | solution.py:35
  92.0 14.1 %collective-permute-start.5 = (bf16[192,1024]{1,0:T(8,128)(2,1)}, bf16[192,1024]{1,0:T(8,128)(2,1)}, u32[]{:S(2)}, u32[]{:S(2)}) collective-permute-start(bf16[192,1024]{1,0:T(8,128)(2,1)} %collective-permute-done.4), channel_id=1, source_target_pairs={{0,8},{8,16},{16,24},{24,32},{32,40},{40,48},{48,56},{56,0},{1,9},... | collective-permute-start | bytes 1179656 | tf_op jit(solution)/shard_map/ppermute | solution.py:32
  98.1 13.6 %collective-permute-start.2 = (bf16[192,1024]{1,0:T(8,128)(2,1)}, bf16[192,1024]{1,0:T(8,128)(2,1)S(1)}, u32[]{:S(2)}, u32[]{:S(2)}) collective-permute-start(bf16[192,1024]{1,0:T(8,128)(2,1)} %collective-permute-done.1), channel_id=1, source_target_pairs={{0,56},{8,0},{16,8},{24,16},{32,24},{40,32},{48,40},{56,48},{1,57}... | collective-permute-start | bytes 1179656 | tf_op jit(solution)/shard_map/ppermute | solution.py:35
  106.1 9.9 %collective-permute-start.6 = (bf16[192,1024]{1,0:T(8,128)(2,1)}, bf16[192,1024]{1,0:T(8,128)(2,1)S(1)}, u32[]{:S(2)}, u32[]{:S(2)}) collective-permute-start(bf16[192,1024]{1,0:T(8,128)(2,1)} %collective-permute-done.5), channel_id=1, source_target_pairs={{0,8},{8,16},{16,24},{24,32},{32,40},{40,48},{48,56},{56,0},{1,9},... | collective-permute-start | bytes 1179656 | tf_op jit(solution)/shard_map/ppermute | solution.py:32
  125.4 2.4 copy-start.4
  158.1 22.8 %copy-start.5 = (s32[1,192,2]{1,2,0:T(2,128)S(1)}, s32[1,192,2]{1,2,0:T(2,128)}, u32[]{:S(2)}) copy-start(s32[1,192,2]{1,2,0:T(2,128)} %param.16) | copy-start | bytes 4612
  160.6 0.7 copy-start.3
  162.0 29.5 %copy-start.1 = (bf16[1,192,1024]{2,1,0:T(8,128)(2,1)S(1)}, bf16[1,192,1024]{2,1,0:T(8,128)(2,1)}, u32[]{:S(2)}) copy-start(bf16[1,192,1024]{2,1,0:T(8,128)(2,1)} %param.11) | copy-start | bytes 1179652
  162.0 29.5 %copy-start.6 = (f32[1024]{0:T(1024)S(1)}, f32[1024]{0:T(1024)}, u32[]{:S(2)}) copy-start(f32[1024]{0:T(1024)} %param.15) | copy-start | bytes 12292
  172.0 16.2 %all-to-all-start = ((bf16[8,192,128]{2,1,0:T(8,128)(2,1)}), bf16[8,192,128]{2,1,0:T(8,128)(2,1)S(1)}, u32[]{:S(2)}, u32[]{:S(2)}) async-start(bf16[8,192,128]{2,1,0:T(8,128)(2,1)} %fusion.54), calls=%async_computation | async-start | bytes 786432 | tf_op jit(solution)/shard_map/all_to_all | solution.py:72
  188.2 0.7 copy-start.2
  260.2 3.3 copy-start.8
  265.7 13.3 %copy-start.7 = (f32[1,192,2]{1,2,0:T(2,128)S(1)}, f32[1,192,2]{1,2,0:T(2,128)}, u32[]{:S(2)}) copy-start(f32[1,192,2]{1,2,0:T(2,128)} %param.17) | copy-start | bytes 4612
  269.3 62.6 %all-to-all-start.2 = ((bf16[64,12,1024]{2,1,0:T(8,128)(2,1)}), bf16[64,12,1024]{2,1,0:T(8,128)(2,1)}, u32[]{:S(2)}, u32[]{:S(2)}) async-start(bf16[64,12,1024]{2,1,0:T(8,128)(2,1)} %reshape.170), calls=%async_computation.2 | async-start | bytes 4194304 | tf_op jit(solution)/shard_map/all_to_all | solution.py:104
Sparse Core Ops, SparseCore 0:
  47.2 42.2 all-gather.3
